TPU v7x, 256 devices: a whole 4x4x8 slice. The times are simulated.
256 devices in a mesh: req: 64 (over y, z_lo, x, core), tp: 4 (over z_hi).
Axes of the slice: x: 4, y: 4, z: 8 (z_hi: 4, z_lo: 2; z = z_hi * 2 + z_lo), core: 2. Of those that a mesh axis runs over, the one named last changes fastest.
Arguments:
- tokens: bfloat16 [16384, 2048], P('req'), may hold values from -6 to 6
- norm_gain: float32 [2048], replicated, may hold values from 0.25 to 1.75
- w_query: bfloat16 [2048, 2048], P(None, 'tp'), may hold values from -1 to 1
- w_key: bfloat16 [2048, 2048], P(None, 'tp'), may hold values from -1 to 1
- w_value: bfloat16 [2048, 2048], P(None, 'tp'), may hold values from -0.125 to 0.125
- w_out: bfloat16 [2048, 2048], P('tp'), may hold values from -0.125 to 0.125
- lambdas: float32 [4, 8, 128], P(None, 'tp'), may hold values from -1 to 1
- sub_gain: float32 [8, 256], P('tp'), may hold values from 0.5 to 2
- lengths: int32 [4], replicated, may hold values from 1 to 8192, 16384 in all
Outputs:
- hidden: bfloat16 [16384, 2048], P('req')
- key_cache: bfloat16 [16384, 2048], P('req', 'tp')
- value_cache: bfloat16 [16384, 2048], P('req', 'tp')
Inputs may be any that keep to these rules, and one draw needn't show every extreme that they name: The lengths sum to 16384; the longest is exactly 8192.
All inputs are finite; a program needn't handle non-finite values.
Results may differ from a plain program's by a relative error of at most 0.007.
Values may be sent and summed in bfloat16 or wider, within the bound.
No kernel may reach another device: no remote copies, remote signals or barrier semaphores. Data moves between devices by JAX's collectives and lax.ppermute only.
A program may use at most 128 MiB of HBM per device.

v0:
```python
import math
import jax
import jax.numpy as jnp
from jax import lax
from jax.sharding import Mesh
from jax.sharding import PartitionSpec as P

QK = 128
VD = 256
MAXLEN = 8192
lambda_start = 0.8 - 0.6 * math.exp(-3.3)
masked_score = -1e30


def locate(index, lengths):
    ends = jnp.cumsum(lengths)
    starts = ends - lengths
    segment = jnp.sum((ends[None, :] <= index[:, None]).astype(jnp.int32), axis=1)
    hit = jnp.arange(lengths.shape[0], dtype=jnp.int32)[None, :] == segment[:, None]
    begin = jnp.sum(jnp.where(hit, starts[None, :], 0), axis=1)
    return (segment, index - begin)


def rotate(proj, position):
    half = proj.shape[-1] // 2
    freq = 10000.0 ** (-jnp.arange(half, dtype=jnp.float32) / half)
    angle = position.astype(jnp.float32)[:, None] * freq[None, :]
    cosine = jnp.cos(angle)[:, None, None, :]
    sine = jnp.sin(angle)[:, None, None, :]
    front = proj[..., :half]
    back = proj[..., half:]
    return jnp.concatenate([front * cosine - back * sine, back * cosine + front * sine], axis=-1)


def swap_cores(value):
    return lax.ppermute(value, "core", [(0, 1), (1, 0)])


def on_device(tokens, norm_gain, w_query, w_key, w_value, w_out, lambdas, sub_gain, lengths):
    rows = tokens.shape[0]
    heads = w_query.shape[1] // (2 * QK)
    key_cols = heads * 2 * QK
    ys, zs, xs = (lax.axis_size("y"), lax.axis_size("z"), lax.axis_size("x"))
    chips = ys * zs * xs
    total = rows * 2 * chips
    core = lax.axis_index("core")
    chip = (lax.axis_index("y") * zs + lax.axis_index("z")) * xs + lax.axis_index("x")
    first = (chip * 2 + core) * rows
    local_index = first + jnp.arange(rows, dtype=jnp.int32)
    unused, pos_own = locate(local_index, lengths)
    xf = tokens.astype(jnp.float32)
    normed = (xf * lax.rsqrt(jnp.mean(xf * xf, axis=-1, keepdims=True) + 1e-06) * norm_gain).astype(
        jnp.bfloat16
    )
    keys = rotate(
        jnp.dot(normed, w_key, preferred_element_type=jnp.float32).reshape(rows, heads, 2, QK),
        pos_own,
    ).astype(jnp.bfloat16)
    values = jnp.dot(normed, w_value, preferred_element_type=jnp.float32).astype(jnp.bfloat16)
    key_flat = keys.reshape(rows, key_cols)
    lam = (
        jnp.exp(jnp.sum(lambdas[0] * lambdas[1], axis=-1))
        - jnp.exp(jnp.sum(lambdas[2] * lambdas[3], axis=-1))
        + lambda_start
    )
    scale = QK ** (-0.5)

    def head_kv(h):
        k_h = lax.dynamic_index_in_dim(keys, h, axis=1, keepdims=False).reshape(rows, 2 * QK)
        v_h = lax.dynamic_index_in_dim(values.reshape(rows, heads, VD), h, axis=1, keepdims=False)
        return jnp.concatenate([k_h, v_h], axis=1)

    def in_order(mine, theirs, first_is_mine):
        rows_each = mine.shape[0]
        both = jnp.zeros((2 * rows_each,) + mine.shape[1:], mine.dtype)
        both = lax.dynamic_update_slice_in_dim(
            both, mine, jnp.where(first_is_mine, 0, rows_each), axis=0
        )
        return lax.dynamic_update_slice_in_dim(
            both, theirs, jnp.where(first_is_mine, rows_each, 0), axis=0
        )

    span = 2 * rows
    z = lax.axis_index("z")
    kv_both = jnp.stack([head_kv(0), head_kv(1)], axis=1)
    halves = [
        lax.ppermute(kv_both[..., i * 2 * QK : (i + 1) * 2 * QK], "z", [(0, 1), (1, 0)])
        for i in range(2)
    ]
    kv_chips = in_order(kv_both, jnp.concatenate(halves, axis=-1), z == 0)
    mine = lax.dynamic_index_in_dim(kv_chips, core, axis=1, keepdims=False).reshape(2, rows, -1)
    theirs = swap_cores(
        lax.dynamic_index_in_dim(kv_chips, 1 - core, axis=1, keepdims=False)
    ).reshape(2, rows, -1)
    quad = jnp.zeros((2, span, mine.shape[-1]), mine.dtype)
    quad = lax.dynamic_update_slice_in_dim(quad, mine, core * rows, axis=1)
    quad = lax.dynamic_update_slice_in_dim(quad, theirs, (1 - core) * rows, axis=1)
    kv_quad = quad.reshape(2 * span, -1)
    kv_pair = lax.dynamic_index_in_dim(quad, z, axis=0, keepdims=False)
    gathered = lax.all_gather(kv_quad, ("y", "x"), axis=0, tiled=True)
    query = rotate(
        jnp.dot(normed, w_query, preferred_element_type=jnp.float32).reshape(rows, heads, 2, QK),
        pos_own,
    ).astype(jnp.bfloat16)
    q_pair = in_order(
        lax.dynamic_index_in_dim(query, core, axis=1, keepdims=False),
        swap_cores(lax.dynamic_index_in_dim(query, 1 - core, axis=1, keepdims=False)),
        core == 0,
    )
    reach = min(MAXLEN // span, chips - 1)
    window = reach * span
    base = chip * span
    first_chip = jnp.clip(chip - reach, 0, chips - reach)
    start = first_chip * span
    q_index = base + jnp.arange(span, dtype=jnp.int32)
    q_seg, unused = locate(q_index, lengths)

    def stats_of(kv_win, key_index, allowed):
        v_win = kv_win[:, 2 * QK :]
        stats = []
        for m in range(2):
            k_m = kv_win[:, m * QK : (m + 1) * QK]
            scores = (
                jnp.einsum("qd,kd->qk", q_pair[:, m, :], k_m, preferred_element_type=jnp.float32)
                * scale
            )
            scores = jnp.where(allowed, scores, masked_score)
            top = jnp.max(scores, axis=-1, keepdims=True)
            weights = jnp.where(allowed, jnp.exp(scores - top), 0.0)
            mass = jnp.sum(weights, axis=-1, keepdims=True)
            acc = jnp.dot(weights.astype(jnp.bfloat16), v_win, preferred_element_type=jnp.float32)
            stats.append((top, mass, acc))
        return stats

    local_allowed = (q_index[None, :] <= q_index[:, None]) & (q_seg[None, :] == q_seg[:, None])
    local_stats = stats_of(kv_pair, q_index, local_allowed)
    local_stats, gathered = lax.optimization_barrier((local_stats, gathered))
    c = first_chip + jnp.arange(reach, dtype=jnp.int32)
    slot = (c // (zs * xs) * xs + c % xs) * zs + c // xs % zs
    kv_window = jnp.take(gathered.reshape(chips, span, -1), slot, axis=0, mode="clip").reshape(
        window, -1
    )
    pieces = 2
    piece = window // pieces

    def part(p):
        key_index = start + p * piece + jnp.arange(piece, dtype=jnp.int32)
        k_seg, unused = locate(key_index, lengths)
        allowed = (key_index[None, :] < base) & (k_seg[None, :] == q_seg[:, None])
        return stats_of(kv_window[p * piece : (p + 1) * piece], key_index, allowed)

    all_stats = [local_stats] + [part(p) for p in range(pieces)]

    def attend(m):
        tops = [stats[m][0] for stats in all_stats]
        top = tops[0]
        for other in tops[1:]:
            top = jnp.maximum(top, other)
        acc = 0.0
        mass = 0.0
        for stats in all_stats:
            fade = jnp.exp(stats[m][0] - top)
            mass = mass + stats[m][1] * fade
            acc = acc + stats[m][2] * fade
        return acc / mass

    lam_h = lax.dynamic_index_in_dim(lam, core, keepdims=False)
    gain_h = lax.dynamic_index_in_dim(sub_gain, core, axis=0, keepdims=False)
    diff = attend(0) - lam_h * attend(1)
    head_out = (
        diff
        * lax.rsqrt(jnp.mean(diff * diff, axis=-1, keepdims=True) + 1e-05)
        * gain_h
        * (1.0 - lambda_start)
    ).astype(jnp.bfloat16)
    own_rows = lax.dynamic_slice_in_dim(head_out, core * rows, rows, axis=0)
    other_rows = swap_cores(lax.dynamic_slice_in_dim(head_out, (1 - core) * rows, rows, axis=0))
    merged = jnp.where(
        core == 0,
        jnp.concatenate([own_rows, other_rows], axis=1),
        jnp.concatenate([other_rows, own_rows], axis=1),
    )
    summed = lax.psum(
        jnp.dot(merged, w_out, preferred_element_type=jnp.float32).astype(jnp.bfloat16), "tp"
    ).astype(jnp.float32)
    hidden = (xf + summed).astype(jnp.bfloat16)
    return (hidden, key_flat, values)


def solution(mesh):
    req, tp = (mesh.shape["req"], mesh.shape["tp"])
    paired = Mesh(mesh.devices.reshape(req // 16, 2, 4, 2, tp), ("y", "z", "x", "core", "tp"))
    rows = ("y", "z", "x", "core")
    in_specs = (
        P(rows, None),
        P(),
        P(None, "tp"),
        P(None, "tp"),
        P(None, "tp"),
        P("tp", None),
        P(None, "tp", None),
        P("tp", None),
        P(),
    )
    out_specs = (P(rows, None), P(rows, "tp"), P(rows, "tp"))
    return jax.shard_map(
        on_device, mesh=paired, in_specs=in_specs, out_specs=out_specs, check_vma=False
    )
```

profile of v0, /device:TPU:1, one launch (start us, length us, event | category | flops | bytes accessed | tf_op | source)
XLA Modules:
  0.0 296.7 jit_solution(17206890886922927815)
XLA Ops:
  9.1 1.5 fusion.16
  10.6 2.7 fusion.131
  16.6 2.7 convolution_convert_fusion.1
  22.2 2.5 collective-permute-start.1
  24.8 5.1 %collective-permute-done.1 = bf16[256,2,256]{2,0,1:T(8,128)(2,1)S(1)} collective-permute-done((bf16[256,2,256]{2,0,1:T(8,128)(2,1)}, bf16[256,2,256]{2,0,1:T(8,128)(2,1)S(1)}, u32[]{:S(2)}, u32[]{:S(2)}) %collective-permute-start.1) | collective-permute-done | bytes 262176 | tf_op jit(solution)/shard_map/ppermute | solution.py:87
  30.0 5.5 %collective-permute-done.2 = bf16[256,2,256]{2,0,1:T(8,128)(2,1)} collective-permute-done((bf16[256,2,256]{2,0,1:T(8,128)(2,1)S(1)}, bf16[256,2,256]{2,0,1:T(8,128)(2,1)}, u32[]{:S(2)}, u32[]{:S(2)}) %collective-permute-start.2) | collective-permute-done | bytes 262176 | tf_op jit(solution)/shard_map/ppermute | solution.py:87
  37.5 2.4 collective-permute-start.3
  40.0 1.1 constant_dynamic-update-slice_fusion.1
  43.9 3.6 %fusion.133 = f32[256,512]{1,0:T(8,128)} fusion(bf16[2048,512]{1,0:T(8,128)(2,1)} %param.11, bf16[256,2048]{1,0:T(8,128)(2,1)} %param.9, f32[2048]{0:T(1024)S(1)} %copy-done.16, f32[256]{0:T(256)S(1)} %add_rsqrt_fusion.1), kind=kOutput, calls=%fused_computation.180 | convolution fusion | flops 538968064 | bytes 3679232 | tf_op jit(solution)/shard_map/dot_general | solution.py:102
  47.5 2.2 reshape.336
  49.7 2.0 add_convert_fusion
  56.0 1.3 convert_reduce_fusion.2
  59.3 1.2 dynamic_slice.55
  61.3 1.6 constant_dynamic-update-slice_fusion.2
  63.0 1.3 fusion.139
  64.3 1.3 fusion.138
  66.6 1.4 fusion.97
  68.0 94.9 %all-gather.2.cloned.1.call-done = bf16[16384,512]{1,0:T(8,128)(2,1)} async-done(((bf16[1024,512]{1,0:T(8,128)(2,1)}), bf16[16384,512]{1,0:T(8,128)(2,1)}) %all-gather.2.cloned.1.call-update) | async-done | bytes 16777232 | tf_op jit(solution)/shard_map/all_gather | solution.py:100
  162.8 10.7 %gather_fusion = bf16[16,512,512]{2,1,0:T(8,128)(2,1)} fusion(bf16[32,512,512]{2,1,0:T(8,128)(2,1)} %bitcast.87, s32[1024]{0:T(1024)} %pad_clamp_fusion), kind=kCustom, calls=%fused_computation | custom fusion | bytes 16777280 | tf_op jit(solution)/shard_map/jit(_take)/gather | solution.py:140
  173.5 3.9 %fusion.135 = (bf16[8,512,512]{2,1,0:T(8,128)(2,1)S(1)}, bf16[8,512,512]{2,1,0:T(8,128)(2,1)S(1)}) fusion(bf16[16,512,512]{2,1,0:T(8,128)(2,1)} %gather_fusion), kind=kLoop, calls=%fused_computation.181 | loop fusion | bytes 16777216 | tf_op jit(solution)/shard_map/slice | solution.py:150
  177.4 2.4 fusion.142
  179.8 2.4 fusion.141
  182.2 4.6 %fusion.143 = (f32[512]{0:T(512)S(1)}, f32[512,4096]{1,0:T(8,128)}) fusion(bf16[4096,512]{1,0:T(8,128)(2,1)S(1)} %bitcast.92, bf16[512,2,128]{2,0,1:T(8,128)(2,1)S(1)} %copy-done.8, s32[512]{0:T(512)S(1)} %copy-done.9, s32[4096]{0:T(1024)S(1)} %get-tuple-element.28, pred[4096]{0:T(1024)(128)(4,1)S(1)} %copy-done.13), kind=kOutput, calls=%fused_computation.189 | convolution fusion | flops 547356160 | bytes 9592832 | tf_op jit(solution)/shard_map/qd,kd->qk/dot_general | solution.py:124
  186.8 3.6 %fusion.140 = (f32[512]{0:T(512)S(1)}, f32[512,4096]{1,0:T(8,128)S(1)}) fusion(bf16[4096,512]{1,0:T(8,128)(2,1)} %bitcast.93, bf16[512,2,128]{2,0,1:T(8,128)(2,1)S(1)} %copy-done.8, s32[512]{0:T(512)S(1)} %copy-done.9, s32[4096]{0:T(1024)S(1)} %get-tuple-element.28, pred[4096]{0:T(1024)(128)(4,1)S(1)} %copy-done.13), kind=kOutput, calls=%fused_computation.186 | convolution fusion | flops 547356160 | bytes 9592832 | tf_op jit(solution)/shard_map/qd,kd->qk/dot_general | solution.py:124
  190.4 11.0 %fusion.4 = (f32[512]{0:T(512)S(1)}, f32[512]{0:T(512)S(1)}, f32[512]{0:T(512)S(1)}, f32[512]{0:T(512)S(1)}) fusion(f32[512,4096]{1,0:T(8,128)S(1)} %get-tuple-element.64, f32[512]{0:T(512)S(1)} %get-tuple-element.63, s32[4096]{0:T(1024)S(1)} %get-tuple-element.27, s32[512]{0:T(512)S(1)} %copy-done.9, pred[4096]{0:T(1024)(128)(4,1)S(1)} %copy-done.12, ...), kind=kLoop, calls=%fused_computation.15 | loop fusion | flops 33552384 | bytes 33613824 | tf_op jit(solution)/shard_map/reduce_sum | solution.py:130
  201.4 5.6 %fusion.61 = f32[512,256]{1,0:T(8,128)S(1)} fusion(bf16[4096,512]{1,0:T(8,128)(2,1)} %bitcast.94, f32[512,4096]{1,0:T(8,128)} %get-tuple-element.68, f32[512]{0:T(512)S(1)} %get-tuple-element.67, s32[4096]{0:T(1024)S(1)} %get-tuple-element.28, s32[512]{0:T(512)S(1)} %copy-done.9, pred[4096]{0:T(1024)(128)(4,1)S(1)} %copy-done.13, f32[512]{0:T(512)S(1)} %bitcast.124), kind=kOutput, calls=%fused_computation.46 | convolution fusion | flops 1084358656 | bytes 11036672 | tf_op jit(solution)/shard_map/dot_general | solution.py:131
  207.1 3.9 %fusion.41 = f32[512,256]{1,0:T(8,128)S(1)} fusion(bf16[4096,512]{1,0:T(8,128)(2,1)} %bitcast.95, f32[512,4096]{1,0:T(8,128)S(1)} %get-tuple-element.62, f32[512]{0:T(512)S(1)} %get-tuple-element.61, s32[4096]{0:T(1024)S(1)} %get-tuple-element.28, s32[512]{0:T(512)S(1)} %copy-done.9, pred[4096]{0:T(1024)(128)(4,1)S(1)} %copy-done.13, f32[512]{0:T(512)S(1)} %bitcast.123), kind=kOutput, calls=%fused_computation.42 | convolution fusion | flops 1084358656 | bytes 11036672 | tf_op jit(solution)/shard_map/dot_general | solution.py:131
  211.1 2.4 fusion.85
  213.4 3.1 %multiply_reduce_fusion = (f32[512]{0:T(512)S(1)}, f32[512,256]{1,0:T(8,128)S(1)}) fusion(f32[512,256]{1,0:T(8,128)S(1)} %fusion.85, f32[512]{0:T(512)S(1)} %bitcast.117, f32[512,256]{1,0:T(8,128)S(1)} %fusion.61, f32[512]{0:T(512)S(1)} %bitcast.119, bf16[4096,512]{1,0:T(8,128)(2,1)S(1)} %bitcast.91, f32[512,4096]{1,0:T(8,128)S(1)} %get-tuple-element.64, ...), kind=kOutput, calls=%fused_computation.74 | convolution fusion | flops 1085406720 | bytes 12615684 | tf_op jit(solution)/shard_map/dot_general | solution.py:131
  218.5 1.7 convolution_convert_fusion
  221.0 66.2 %all-reduce.2.cloned.1.call-done = bf16[256,2048]{1,0:T(8,128)(2,1)} async-done(((bf16[256,2048]{1,0:T(8,128)(2,1)}), bf16[256,2048]{1,0:T(8,128)(2,1)}) %all-reduce.2.cloned.1.call-update) | async-done | bytes 1048592 | tf_op jit(solution)/shard_map/psum | solution.py:183
  287.2 2.6 fusion.19
  (96 shorter events, 24.1 us)
Async XLA Ops:
  7.2 211.3 %copy-start = (bf16[512,2048]{1,0:T(8,128)(2,1)S(1)}, bf16[512,2048]{1,0:T(8,128)(2,1)}, u32[]{:S(2)}) copy-start(bf16[512,2048]{1,0:T(8,128)(2,1)} %param.14) | copy-start | bytes 6291460
  7.2 155.7 %all-gather.2.cloned.1.call-start = ((), (), s32[]{:S(2)}) async-start(), calls=%async_computation | async-start | bytes 17825792 | tf_op jit(solution)/shard_map/all_gather | solution.py:100
  8.2 2.4 copy-start.14
  10.6 6.0 %copy-start.16 = (f32[2048]{0:T(1024)S(1)}, f32[2048]{0:T(1024)}, u32[]{:S(2)}) copy-start(f32[2048]{0:T(1024)} %param.10) | copy-start | bytes 24580
  14.2 5.9 %copy-start.5 = (f32[256,64]{1,0:T(8,128)}, f32[256,64]{1,0:T(8,128)S(1)}, u32[]{:S(2)}) copy-start(f32[256,64]{1,0:T(8,128)S(1)} %get-tuple-element.56) | copy-start | bytes 196612
  19.3 0.7 copy-start.6
  22.2 7.8 %collective-permute-start.1 = (bf16[256,2,256]{2,0,1:T(8,128)(2,1)}, bf16[256,2,256]{2,0,1:T(8,128)(2,1)S(1)}, u32[]{:S(2)}, u32[]{:S(2)}) collective-permute-start(bf16[256,2,256]{2,0,1:T(8,128)(2,1)} %get-tuple-element.47), channel_id=1, source_target_pairs={{0,32},{32,0},{1,33},{33,1},{2,34},{34,2},{3,35},{35,3},{4,36},{36... | collective-permute-start | bytes 786440 | tf_op jit(solution)/shard_map/ppermute | solution.py:87
  24.7 10.8 %collective-permute-start.2 = (bf16[256,2,256]{2,0,1:T(8,128)(2,1)S(1)}, bf16[256,2,256]{2,0,1:T(8,128)(2,1)}, u32[]{:S(2)}, u32[]{:S(2)}) collective-permute-start(bf16[256,2,256]{2,0,1:T(8,128)(2,1)S(1)} %get-tuple-element.48), channel_id=1, source_target_pairs={{0,32},{32,0},{1,33},{33,1},{2,34},{34,2},{3,35},{35,3},{4,36},{36... | collective-permute-start | bytes 786440 | tf_op jit(solution)/shard_map/ppermute | solution.py:87
  37.5 4.3 %collective-permute-start.3 = (bf16[512,512]{1,0:T(8,128)(2,1)}, bf16[512,512]{1,0:T(8,128)(2,1)}, u32[]{:S(2)}, u32[]{:S(2)}) collective-permute-start(bf16[512,512]{1,0:T(8,128)(2,1)} %get-tuple-element.39), channel_id=1, source_target_pairs={{0,4},{4,0},{1,5},{5,1},{2,6},{6,2},{3,7},{7,3},{8,12},{12,8},{9,1... | collective-permute-start | bytes 1572872 | tf_op jit(solution)/shard_map/ppermute | solution.py:36
  42.9 1.0 copy-start.1
  43.9 11.4 %copy-start.15 = (f32[4,2,128]{2,1,0:T(2,128)S(1)}, f32[4,2,128]{2,1,0:T(2,128)}, u32[]{:S(2)}) copy-start(f32[4,2,128]{2,1,0:T(2,128)} %param.15) | copy-start | bytes 12292
  43.9 19.1 %copy-start.2 = (bf16[2,512,512]{2,1,0:T(8,128)(2,1)S(1)}, bf16[2,512,512]{2,1,0:T(8,128)(2,1)}, u32[]{:S(2)}) copy-start(bf16[2,512,512]{2,1,0:T(8,128)(2,1)} %copy-done.1) | copy-start | bytes 3145732
  43.9 243.3 %all-reduce.2.cloned.1.call-start = ((), (), s32[]{:S(2)}) async-start(), calls=%async_computation.1 | async-start | bytes 2097152 | tf_op jit(solution)/shard_map/psum | solution.py:183
  53.1 8.3 %collective-permute-start = (bf16[256,2,128]{2,0,1:T(8,128)(2,1)}, bf16[256,2,128]{2,0,1:T(8,128)(2,1)}, u32[]{:S(2)}, u32[]{:S(2)}) collective-permute-start(bf16[256,2,128]{2,0,1:T(8,128)(2,1)} %bitcast.85), channel_id=1, source_target_pairs={{0,4},{4,0},{1,5},{5,1},{2,6},{6,2},{3,7},{7,3},{8,12},{12,8},{9,1... | collective-permute-start | bytes 393224 | tf_op jit(solution)/shard_map/ppermute | solution.py:36
  53.5 4.3 %copy-start.10 = (s32[512]{0:T(512)}, s32[512]{0:T(512)S(1)}, u32[]{:S(2)}) copy-start(s32[512]{0:T(512)S(1)} %iota_add_fusion.2) | copy-start | bytes 6148
  57.9 0.7 copy-start.7
  58.6 7.0 %copy-start.9 = (s32[512]{0:T(512)S(1)}, s32[512]{0:T(512)}, u32[]{:S(2)}) copy-start(s32[512]{0:T(512)} %convert_reduce_fusion.2) | copy-start | bytes 6148
  58.6 7.0 %copy-start.11 = (s32[512]{0:T(512)S(1)}, s32[512]{0:T(512)}, u32[]{:S(2)}) copy-start(s32[512]{0:T(512)} %copy-done.10) | copy-start | bytes 6148
  173.5 3.9 %copy-start.8 = (bf16[512,2,128]{2,0,1:T(8,128)(2,1)S(1)}, bf16[512,2,128]{2,0,1:T(8,128)(2,1)}, u32[]{:S(2)}) copy-start(bf16[512,2,128]{2,0,1:T(8,128)(2,1)} %constant_dynamic-update-slice_fusion.2) | copy-start | bytes 786436
  173.5 3.9 %copy-start.12 = (pred[4096]{0:T(1024)(128)(4,1)S(1)}, pred[4096]{0:T(1024)(128)(4,1)}, u32[]{:S(2)}) copy-start(pred[4096]{0:T(1024)(128)(4,1)} %broadcast_compare_fusion.1) | copy-start | bytes 12292
  177.4 4.8 %copy-start.4 = (bf16[8,512,512]{2,1,0:T(8,128)(2,1)}, bf16[8,512,512]{2,1,0:T(8,128)(2,1)S(1)}, u32[]{:S(2)}) copy-start(bf16[8,512,512]{2,1,0:T(8,128)(2,1)S(1)} %get-tuple-element.38) | copy-start | bytes 12582916
  179.8 2.4 copy-start.13
  207.1 4.0 %copy-start.17 = (f32[512,256]{1,0:T(8,128)S(1)}, f32[512,256]{1,0:T(8,128)}, u32[]{:S(2)}) copy-start(f32[512,256]{1,0:T(8,128)} %fusion.97) | copy-start | bytes 1572868
  216.5 70.7 %copy-start.3 = (bf16[256,2048]{1,0:T(8,128)(2,1)S(1)}, bf16[256,2048]{1,0:T(8,128)(2,1)}, u32[]{:S(2)}) copy-start(bf16[256,2048]{1,0:T(8,128)(2,1)} %param.9) | copy-start | bytes 3145732
  216.7 1.8 collective-permute-start.4
Sparse Core Ops, SparseCore 0:
  44.0 118.7 all-gather.1
  220.3 66.8 all-reduce.1
where the time goes:
time: 297 us
  waiting for transfers between devices  173 us (58%)
  matrix products  43.2 us (15%)
  local copies, waits for them, and re-layouts  30.1 us (10%)
  other arithmetic  29.3 us (10%)
  between operations  14.5 us (5%)
  starting transfers between devices  6.13 us (2%)
    all_gather x1, waiting for transfers between devices, on_device(): gathered = lax.all_gather(kv_quad, ('y', 'x'), axis=0, tiled=True)  94.9 us
    psum x1, waiting for transfers between devices, on_device(): lax.psum(jnp.dot(merged, w_out, preferred_element_type=jnp.float32).astyp...  66.2 us
    dot_general x6, matrix products, stats_of(): jnp.dot(weights.astype(jnp.bfloat16), v_win, preferred_element_type=jnp.f...  17 us
    dot_general x6, matrix products, stats_of(): jnp.einsum('qd,kd->qk', q_pair[:, m, :], k_m, preferred_element_type=jnp....  15.6 us
    reduce_sum x2, other arithmetic, stats_of(): mass = jnp.sum(weights, axis=-1, keepdims=True)  11.4 us
    gather x1, local copies, waits for them, and re-layouts, on_device(): jnp.take(gathered.reshape(chips, span, -1), slot, axis=0, mode='clip')  10.7 us
    ppermute x2, waiting for transfers between devices, on_device(): lax.ppermute(kv_both[..., i * 2 * QK:(i + 1) * 2 * QK], 'z', [(0, 1), (1,...  10.6 us
  transfers between devices with their start and end apart: 7, of which 6 were waited for; matrix products, arithmetic and copies ran while one was open for 8% of the time, Pallas kernels for 0%

commit v1 on v0

--- a/solution.py
+++ b/solution.py
@@ -180,7 +180,8 @@
         jnp.concatenate([own_rows, other_rows], axis=1),
         jnp.concatenate([other_rows, own_rows], axis=1),
     )
-    summed = lax.psum(
+    recover_scenes = lambda s0, axis_tag: jnp.sum(lax.all_gather(s0, axis_tag), 0)
+    summed = recover_scenes(
         jnp.dot(merged, w_out, preferred_element_type=jnp.float32).astype(jnp.bfloat16), "tp"
     ).astype(jnp.float32)
     hidden = (xf + summed).astype(jnp.bfloat16)

time: 297 us -> 320 us (1.077)
  the two profiles are of different devices: /device:TPU:1 before, /device:TPU:37 now
where the time goes in v1:
time: 320 us; the launch traced here: 319 us
  waiting for transfers between devices  194 us (61%)
  matrix products  43.2 us (14%)
  other arithmetic  33.5 us (10%)
  local copies, waits for them, and re-layouts  30.1 us (9%)
  between operations  14.5 us (5%)
  starting transfers between devices  4.22 us (1%)
    all_gather x1, waiting for transfers between devices, on_device(): gathered = lax.all_gather(kv_quad, ('y', 'x'), axis=0, tiled=True)  94.6 us
    all_gather x1, waiting for transfers between devices, on_device(): lax.all_gather(s0, axis_tag)  85.7 us
    dot_general x6, matrix products, stats_of(): jnp.dot(weights.astype(jnp.bfloat16), v_win, preferred_element_type=jnp.f...  17 us
    dot_general x6, matrix products, stats_of(): jnp.einsum('qd,kd->qk', q_pair[:, m, :], k_m, preferred_element_type=jnp....  15.6 us
    ppermute x2, waiting for transfers between devices, on_device(): lax.ppermute(kv_both[..., i * 2 * QK:(i + 1) * 2 * QK], 'z', [(0, 1), (1,...  11.5 us
    reduce_sum x2, other arithmetic, stats_of(): mass = jnp.sum(weights, axis=-1, keepdims=True)  11.4 us
    gather x1, local copies, waits for them, and re-layouts, on_device(): jnp.take(gathered.reshape(chips, span, -1), slot, axis=0, mode='clip')  10.7 us
  transfers between devices with their start and end apart: 7, of which 6 were waited for; matrix products, arithmetic and copies ran while one was open for 8% of the time, Pallas kernels for 0%

profile of v1, /device:TPU:37, one launch (start us, length us, event | category | flops | bytes accessed | tf_op | source)
XLA Modules:
  0.0 319.2 jit_solution(12914185535965978246)
XLA Ops:
  9.1 1.5 fusion.16
  10.6 2.7 fusion.131
  16.6 2.7 convolution_convert_fusion.1
  22.2 1.5 collective-permute-start.2
  23.8 5.8 %collective-permute-done.1 = bf16[256,2,256]{2,0,1:T(8,128)(2,1)S(1)} collective-permute-done((bf16[256,2,256]{2,0,1:T(8,128)(2,1)}, bf16[256,2,256]{2,0,1:T(8,128)(2,1)S(1)}, u32[]{:S(2)}, u32[]{:S(2)}) %collective-permute-start.1) | collective-permute-done | bytes 262176 | tf_op jit(solution)/shard_map/ppermute | solution.py:87
  29.6 5.7 %collective-permute-done.2 = bf16[256,2,256]{2,0,1:T(8,128)(2,1)} collective-permute-done((bf16[256,2,256]{2,0,1:T(8,128)(2,1)S(1)}, bf16[256,2,256]{2,0,1:T(8,128)(2,1)}, u32[]{:S(2)}, u32[]{:S(2)}) %collective-permute-start.2) | collective-permute-done | bytes 262176 | tf_op jit(solution)/shard_map/ppermute | solution.py:87
  37.4 1.5 collective-permute-start.3
  43.0 3.6 %fusion.133 = f32[256,512]{1,0:T(8,128)} fusion(bf16[2048,512]{1,0:T(8,128)(2,1)} %param.11, bf16[256,2048]{1,0:T(8,128)(2,1)} %param.9, f32[2048]{0:T(1024)S(1)} %copy-done.16, f32[256]{0:T(256)S(1)} %add_rsqrt_fusion.1), kind=kOutput, calls=%fused_computation.180 | convolution fusion | flops 538968064 | bytes 3679232 | tf_op jit(solution)/shard_map/dot_general | solution.py:102
  46.5 2.2 reshape.336
  48.7 2.0 add_convert_fusion
  55.0 1.3 convert_reduce_fusion.2
  58.3 1.2 dynamic_slice.55
  60.3 1.6 constant_dynamic-update-slice_fusion.2
  62.0 1.3 fusion.139
  63.3 1.3 fusion.138
  65.6 1.4 fusion.97
  67.0 94.6 %all-gather.4.cloned.1.call-done = bf16[16384,512]{1,0:T(8,128)(2,1)} async-done(((bf16[1024,512]{1,0:T(8,128)(2,1)}), bf16[16384,512]{1,0:T(8,128)(2,1)}) %all-gather.4.cloned.1.call-update) | async-done | bytes 16777232 | tf_op jit(solution)/shard_map/all_gather | solution.py:100
  161.6 10.7 %gather_fusion = bf16[16,512,512]{2,1,0:T(8,128)(2,1)} fusion(bf16[32,512,512]{2,1,0:T(8,128)(2,1)} %bitcast.88, s32[1024]{0:T(1024)} %pad_clamp_fusion), kind=kCustom, calls=%fused_computation | custom fusion | bytes 16777280 | tf_op jit(solution)/shard_map/jit(_take)/gather | solution.py:140
  172.3 3.9 %fusion.135 = (bf16[8,512,512]{2,1,0:T(8,128)(2,1)S(1)}, bf16[8,512,512]{2,1,0:T(8,128)(2,1)S(1)}) fusion(bf16[16,512,512]{2,1,0:T(8,128)(2,1)} %gather_fusion), kind=kLoop, calls=%fused_computation.181 | loop fusion | bytes 16777216 | tf_op jit(solution)/shard_map/slice | solution.py:150
  176.2 2.4 fusion.142
  178.6 2.4 fusion.141
  180.9 4.6 %fusion.143 = (f32[512]{0:T(512)S(1)}, f32[512,4096]{1,0:T(8,128)}) fusion(bf16[4096,512]{1,0:T(8,128)(2,1)S(1)} %bitcast.94, bf16[512,2,128]{2,0,1:T(8,128)(2,1)S(1)} %copy-done.8, s32[512]{0:T(512)S(1)} %copy-done.9, s32[4096]{0:T(1024)S(1)} %get-tuple-element.28, pred[4096]{0:T(1024)(128)(4,1)S(1)} %copy-done.13), kind=kOutput, calls=%fused_computation.189 | convolution fusion | flops 547356160 | bytes 9592832 | tf_op jit(solution)/shard_map/qd,kd->qk/dot_general | solution.py:124
  185.6 3.6 %fusion.140 = (f32[512]{0:T(512)S(1)}, f32[512,4096]{1,0:T(8,128)S(1)}) fusion(bf16[4096,512]{1,0:T(8,128)(2,1)} %bitcast.95, bf16[512,2,128]{2,0,1:T(8,128)(2,1)S(1)} %copy-done.8, s32[512]{0:T(512)S(1)} %copy-done.9, s32[4096]{0:T(1024)S(1)} %get-tuple-element.28, pred[4096]{0:T(1024)(128)(4,1)S(1)} %copy-done.13), kind=kOutput, calls=%fused_computation.186 | convolution fusion | flops 547356160 | bytes 9592832 | tf_op jit(solution)/shard_map/qd,kd->qk/dot_general | solution.py:124
  189.2 11.0 %fusion.4 = (f32[512]{0:T(512)S(1)}, f32[512]{0:T(512)S(1)}, f32[512]{0:T(512)S(1)}, f32[512]{0:T(512)S(1)}) fusion(f32[512,4096]{1,0:T(8,128)S(1)} %get-tuple-element.64, f32[512]{0:T(512)S(1)} %get-tuple-element.63, s32[4096]{0:T(1024)S(1)} %get-tuple-element.27, s32[512]{0:T(512)S(1)} %copy-done.9, pred[4096]{0:T(1024)(128)(4,1)S(1)} %copy-done.12, ...), kind=kLoop, calls=%fused_computation.15 | loop fusion | flops 33552384 | bytes 33613824 | tf_op jit(solution)/shard_map/reduce_sum | solution.py:130
  200.1 5.6 %fusion.61 = f32[512,256]{1,0:T(8,128)S(1)} fusion(bf16[4096,512]{1,0:T(8,128)(2,1)} %bitcast.96, f32[512,4096]{1,0:T(8,128)} %get-tuple-element.68, f32[512]{0:T(512)S(1)} %get-tuple-element.67, s32[4096]{0:T(1024)S(1)} %get-tuple-element.28, s32[512]{0:T(512)S(1)} %copy-done.9, pred[4096]{0:T(1024)(128)(4,1)S(1)} %copy-done.13, f32[512]{0:T(512)S(1)} %bitcast.126), kind=kOutput, calls=%fused_computation.46 | convolution fusion | flops 1084358656 | bytes 11036672 | tf_op jit(solution)/shard_map/dot_general | solution.py:131
  205.8 3.9 %fusion.41 = f32[512,256]{1,0:T(8,128)S(1)} fusion(bf16[4096,512]{1,0:T(8,128)(2,1)} %bitcast.97, f32[512,4096]{1,0:T(8,128)S(1)} %get-tuple-element.62, f32[512]{0:T(512)S(1)} %get-tuple-element.61, s32[4096]{0:T(1024)S(1)} %get-tuple-element.28, s32[512]{0:T(512)S(1)} %copy-done.9, pred[4096]{0:T(1024)(128)(4,1)S(1)} %copy-done.13, f32[512]{0:T(512)S(1)} %bitcast.125), kind=kOutput, calls=%fused_computation.42 | convolution fusion | flops 1084358656 | bytes 11036672 | tf_op jit(solution)/shard_map/dot_general | solution.py:131
  209.8 2.4 fusion.85
  212.2 3.1 multiply_reduce_fusion
  217.2 1.7 convolution_convert_fusion
  219.8 85.7 %all-gather.6.cloned.1.call-done = bf16[1024,2048]{1,0:T(8,128)(2,1)} async-done(((bf16[256,2048]{1,0:T(8,128)(2,1)}), bf16[1024,2048]{1,0:T(8,128)(2,1)}) %all-gather.6.cloned.1.call-update) | async-done | bytes 4194320 | tf_op jit(solution)/shard_map/all_gather | solution.py:183
  305.5 4.2 %reduce_sum.162 = bf16[256,2048]{1,0:T(8,128)(2,1)} reduce(bf16[4,256,2048]{2,1,0:T(8,128)(2,1)} %bitcast.89, bf16[]{:T(256)} %constant.140.clone.1), dimensions={0}, to_apply=%region_22.23 | reduce | flops 1572864 | bytes 5242882 | tf_op jit(solution)/shard_map/reduce_sum | solution.py:183
  309.7 2.6 fusion.19
  (97 shorter events, 25.1 us)
Async XLA Ops:
  7.2 210.1 %copy-start = (bf16[512,2048]{1,0:T(8,128)(2,1)S(1)}, bf16[512,2048]{1,0:T(8,128)(2,1)}, u32[]{:S(2)}) copy-start(bf16[512,2048]{1,0:T(8,128)(2,1)} %param.14) | copy-start | bytes 6291460
  7.2 154.4 %all-gather.4.cloned.1.call-start = ((), (), s32[]{:S(2)}) async-start(), calls=%async_computation | async-start | bytes 17825792 | tf_op jit(solution)/shard_map/all_gather | solution.py:100
  8.2 2.4 copy-start.14
  10.6 6.0 %copy-start.16 = (f32[2048]{0:T(1024)S(1)}, f32[2048]{0:T(1024)}, u32[]{:S(2)}) copy-start(f32[2048]{0:T(1024)} %param.10) | copy-start | bytes 24580
  14.2 5.9 %copy-start.5 = (f32[256,64]{1,0:T(8,128)}, f32[256,64]{1,0:T(8,128)S(1)}, u32[]{:S(2)}) copy-start(f32[256,64]{1,0:T(8,128)S(1)} %get-tuple-element.56) | copy-start | bytes 196612
  19.3 0.7 copy-start.6
  22.2 7.4 %collective-permute-start.1 = (bf16[256,2,256]{2,0,1:T(8,128)(2,1)}, bf16[256,2,256]{2,0,1:T(8,128)(2,1)S(1)}, u32[]{:S(2)}, u32[]{:S(2)}) collective-permute-start(bf16[256,2,256]{2,0,1:T(8,128)(2,1)} %get-tuple-element.47), channel_id=1, source_target_pairs={{0,32},{32,0},{1,33},{33,1},{2,34},{34,2},{3,35},{35,3},{4,36},{36... | collective-permute-start | bytes 786440 | tf_op jit(solution)/shard_map/ppermute | solution.py:87
  22.2 13.1 %collective-permute-start.2 = (bf16[256,2,256]{2,0,1:T(8,128)(2,1)S(1)}, bf16[256,2,256]{2,0,1:T(8,128)(2,1)}, u32[]{:S(2)}, u32[]{:S(2)}) collective-permute-start(bf16[256,2,256]{2,0,1:T(8,128)(2,1)S(1)} %get-tuple-element.48), channel_id=1, source_target_pairs={{0,32},{32,0},{1,33},{33,1},{2,34},{34,2},{3,35},{35,3},{4,36},{36... | collective-permute-start | bytes 786440 | tf_op jit(solution)/shard_map/ppermute | solution.py:87
  37.4 3.4 %collective-permute-start.3 = (bf16[512,512]{1,0:T(8,128)(2,1)}, bf16[512,512]{1,0:T(8,128)(2,1)}, u32[]{:S(2)}, u32[]{:S(2)}) collective-permute-start(bf16[512,512]{1,0:T(8,128)(2,1)} %get-tuple-element.39), channel_id=1, source_target_pairs={{0,4},{4,0},{1,5},{5,1},{2,6},{6,2},{3,7},{7,3},{8,12},{12,8},{9,1... | collective-permute-start | bytes 1572872 | tf_op jit(solution)/shard_map/ppermute | solution.py:36
  41.9 1.0 copy-start.1
  42.9 11.4 %copy-start.15 = (f32[4,2,128]{2,1,0:T(2,128)S(1)}, f32[4,2,128]{2,1,0:T(2,128)}, u32[]{:S(2)}) copy-start(f32[4,2,128]{2,1,0:T(2,128)} %param.15) | copy-start | bytes 12292
  42.9 19.1 %copy-start.2 = (bf16[2,512,512]{2,1,0:T(8,128)(2,1)S(1)}, bf16[2,512,512]{2,1,0:T(8,128)(2,1)}, u32[]{:S(2)}) copy-start(bf16[2,512,512]{2,1,0:T(8,128)(2,1)} %copy-done.1) | copy-start | bytes 3145732
  42.9 262.6 %all-gather.6.cloned.1.call-start = ((), (), s32[]{:S(2)}) async-start(), calls=%async_computation.1 | async-start | bytes 5242880 | tf_op jit(solution)/shard_map/all_gather | solution.py:183
  52.1 8.3 %collective-permute-start = (bf16[256,2,128]{2,0,1:T(8,128)(2,1)}, bf16[256,2,128]{2,0,1:T(8,128)(2,1)}, u32[]{:S(2)}, u32[]{:S(2)}) collective-permute-start(bf16[256,2,128]{2,0,1:T(8,128)(2,1)} %bitcast.86), channel_id=1, source_target_pairs={{0,4},{4,0},{1,5},{5,1},{2,6},{6,2},{3,7},{7,3},{8,12},{12,8},{9,1... | collective-permute-start | bytes 393224 | tf_op jit(solution)/shard_map/ppermute | solution.py:36
  52.5 4.3 %copy-start.10 = (s32[512]{0:T(512)}, s32[512]{0:T(512)S(1)}, u32[]{:S(2)}) copy-start(s32[512]{0:T(512)S(1)} %iota_add_fusion.2) | copy-start | bytes 6148
  56.9 0.7 copy-start.7
  57.6 7.0 %copy-start.9 = (s32[512]{0:T(512)S(1)}, s32[512]{0:T(512)}, u32[]{:S(2)}) copy-start(s32[512]{0:T(512)} %convert_reduce_fusion.2) | copy-start | bytes 6148
  57.6 7.0 %copy-start.11 = (s32[512]{0:T(512)S(1)}, s32[512]{0:T(512)}, u32[]{:S(2)}) copy-start(s32[512]{0:T(512)} %copy-done.10) | copy-start | bytes 6148
  172.2 3.9 %copy-start.8 = (bf16[512,2,128]{2,0,1:T(8,128)(2,1)S(1)}, bf16[512,2,128]{2,0,1:T(8,128)(2,1)}, u32[]{:S(2)}) copy-start(bf16[512,2,128]{2,0,1:T(8,128)(2,1)} %constant_dynamic-update-slice_fusion.2) | copy-start | bytes 786436
  172.3 3.9 %copy-start.12 = (pred[4096]{0:T(1024)(128)(4,1)S(1)}, pred[4096]{0:T(1024)(128)(4,1)}, u32[]{:S(2)}) copy-start(pred[4096]{0:T(1024)(128)(4,1)} %broadcast_compare_fusion.1) | copy-start | bytes 12292
  176.1 4.8 %copy-start.4 = (bf16[8,512,512]{2,1,0:T(8,128)(2,1)}, bf16[8,512,512]{2,1,0:T(8,128)(2,1)S(1)}, u32[]{:S(2)}) copy-start(bf16[8,512,512]{2,1,0:T(8,128)(2,1)S(1)} %get-tuple-element.38) | copy-start | bytes 12582916
  178.5 2.4 copy-start.13
  205.8 4.0 %copy-start.17 = (f32[512,256]{1,0:T(8,128)S(1)}, f32[512,256]{1,0:T(8,128)}, u32[]{:S(2)}) copy-start(f32[512,256]{1,0:T(8,128)} %fusion.97) | copy-start | bytes 1572868
  215.5 1.7 collective-permute-start.4
  218.9 90.8 %copy-start.3 = (bf16[256,2048]{1,0:T(8,128)(2,1)S(1)}, bf16[256,2048]{1,0:T(8,128)(2,1)}, u32[]{:S(2)}) copy-start(bf16[256,2048]{1,0:T(8,128)(2,1)} %param.9) | copy-start | bytes 3145732
Sparse Core Ops, SparseCore 0:
  43.0 118.5 all-gather.3
  219.1 86.3 all-gather.5
